TPU v7x, 256 devices: a whole 4x4x8 slice. The times are simulated.
256 devices in a mesh: stn: 64 (over y, z, core), sec: 4 (over x).
Axes of the slice: x: 4, y: 4, z: 8, core: 2. Of those that a mesh axis runs over, the one named last changes fastest.
Arguments:
- voltages: bfloat16 [2, 1024, 569344], P(None, ('stn', 'sec')), may hold values from -6 to 6
- fir_taps: float32 [12, 4096], replicated, may hold values from -1.75 to 1.75
- cor_channels: int32 [256], replicated, may hold values from 0 to 4095, as said below
- beam_channels: int32 [256], replicated, may hold values from 1 to 4094, as said below
- cor_gain: float32 [256], replicated, as said below
- beam_gain: float32 [256], replicated, as said below
- beam_stations: int32 [16, 512], replicated, may hold values from 0 to 511
- beam_codes: int32 [16, 512], replicated, may hold values from 0 to 255
Outputs:
- visibilities: bfloat16 [256, 2, 1024, 1024], P(('stn', 'sec'))
- beams: bfloat16 [256, 16, 2, 256], P(('stn', 'sec'))
Inputs may be any that keep to these rules, and one draw needn't show every extreme that they name: cor_channels and beam_channels together are 512 distinct transform channels. None of beam_channels appears in cor_channels. `cor_gain`: positive. `beam_gain`: positive.
All inputs are finite; a program needn't handle non-finite values.
Results may differ from a plain program's by a relative error of at most 0.0085.
Values may be sent and summed in bfloat16 or wider, within the bound.
No kernel may reach another device: no remote copies, remote signals or barrier semaphores. Data moves between devices by JAX's collectives and lax.ppermute only.
A program may use at most 128 MiB of HBM per device.

v0:
```python
import math
import jax
import jax.numpy as jnp
from jax import lax
from jax.sharding import PartitionSpec as P

STATIONS = 512
epsilon = 1e-05


def make_tables(channel_of, points):
    sample_index = jnp.arange(points, dtype=jnp.int32)
    phase_turns = channel_of[:, None] * sample_index[None, :] % points
    phase_angle = phase_turns.astype(jnp.float32) * (2.0 * math.pi / points)
    table_scale = 1.0 / math.sqrt(points)
    cos_table = (jnp.cos(phase_angle) * table_scale).astype(jnp.bfloat16)
    sin_table = (jnp.sin(phase_angle) * table_scale).astype(jnp.bfloat16)
    return (cos_table, sin_table)


def make_weights(beam_stations, beam_codes, stations):
    station_ids = jnp.arange(stations, dtype=jnp.int32)
    onehot = (beam_stations[:, :, None] == station_ids[None, None, :]).astype(jnp.float32)
    amplitude = (1 + beam_codes // 64).astype(jnp.float32)
    phase_angle = (beam_codes % 64).astype(jnp.float32) * (2.0 * math.pi / 64.0)
    weight_re = jnp.einsum("bk,bks->bs", amplitude * jnp.cos(phase_angle), onehot)
    weight_im = jnp.einsum("bk,bks->bs", amplitude * jnp.sin(phase_angle), onehot)
    return (weight_re.astype(jnp.bfloat16), weight_im.astype(jnp.bfloat16))


def polyphase(in_block, fir_taps, spectra):
    tap_count, points = fir_taps.shape
    framed = in_block.reshape(in_block.shape[0], in_block.shape[1], -1, points)
    summed = jnp.zeros((framed.shape[0], framed.shape[1], spectra, points), jnp.float32)
    for tap_index in range(tap_count):
        summed = summed + fir_taps[tap_index] * framed[
            :, :, tap_index : tap_index + spectra, :
        ].astype(jnp.float32)
    return summed.astype(jnp.bfloat16)


def contract(left_rows, right_rows):
    contract_dims = (((1,), (1,)), ((), ()))
    return lax.dot_general(left_rows, right_rows, contract_dims, preferred_element_type=jnp.float32)


def spectrum(filtered, cos_table, sin_table, slot_gain):
    inputs_here, spectra, points = (filtered.shape[1], filtered.shape[2], filtered.shape[3])
    real_rows = filtered[0].reshape(inputs_here * spectra, points)
    imag_rows = filtered[1].reshape(inputs_here * spectra, points)
    spec_re = contract(cos_table, real_rows) + contract(sin_table, imag_rows)
    spec_im = contract(cos_table, imag_rows) - contract(sin_table, real_rows)
    combined = jnp.concatenate(
        [spec_re.reshape(-1, inputs_here, spectra), spec_im.reshape(-1, inputs_here, spectra)],
        axis=2,
    )
    return (combined * slot_gain[:, None, None]).astype(jnp.bfloat16)


def form_beams(beam_data, weight_re, weight_im):
    spectra = beam_data.shape[2] // 2
    samples = beam_data.reshape(beam_data.shape[0], -1, 2, beam_data.shape[2])
    with_re = jnp.einsum("bs,jspt->jbpt", weight_re, samples, preferred_element_type=jnp.float32)
    with_im = jnp.einsum("bs,jspt->jbpt", weight_im, samples, preferred_element_type=jnp.float32)
    out_re = with_re[..., :spectra] - with_im[..., spectra:]
    out_im = with_re[..., spectra:] + with_im[..., :spectra]
    return jnp.concatenate([out_re, out_im], axis=3)


def per_device(
    voltages, fir_taps, cor_channels, beam_channels, cor_gain, beam_gain, beam_stations, beam_codes
):
    tap_count, points = fir_taps.shape
    stn_count = lax.axis_size("stn")
    sec_count = lax.axis_size("sec")
    device_count = stn_count * sec_count
    inputs_here = voltages.shape[1]
    spectra = voltages.shape[2] // points - tap_count + 1
    filtered = polyphase(voltages, fir_taps, spectra)
    channel_of = jnp.concatenate([cor_channels, beam_channels])
    slot_gain = jnp.concatenate([cor_gain, beam_gain])
    cos_table, sin_table = make_tables(channel_of, points)
    weight_re, weight_im = make_weights(beam_stations, beam_codes, STATIONS)
    spectra_all = spectrum(filtered, cos_table, sin_table, slot_gain)
    outgoing = spectra_all.reshape(2, stn_count, sec_count, 1, 1, inputs_here, 2 * spectra)
    turned = lax.all_to_all(
        lax.all_to_all(outgoing, "stn", split_axis=1, concat_axis=3, tiled=True),
        "sec",
        split_axis=2,
        concat_axis=4,
        tiled=True,
    )
    received = turned.reshape(2, device_count * inputs_here, 2 * spectra)
    cor_data = received[0]
    beam_data = received[1:2]
    swapped = jnp.concatenate([cor_data[:, spectra:], -cor_data[:, :spectra]], axis=1)
    vis_re = contract(cor_data, cor_data) / spectra
    vis_im = contract(swapped, cor_data) / spectra
    visibilities = jnp.stack([vis_re, vis_im])[None].astype(jnp.bfloat16)
    raw_beams = form_beams(beam_data, weight_re, weight_im)
    local_power = jnp.sum(raw_beams * raw_beams, axis=(0, 2, 3))
    summed_power = lax.psum(local_power, ("stn", "sec"))
    beam_power = summed_power / (device_count * raw_beams.shape[2] * raw_beams.shape[3])
    beams = (raw_beams * lax.rsqrt(beam_power + epsilon)[None, :, None, None]).astype(jnp.bfloat16)
    return (visibilities, beams)


def solution(mesh):
    in_specs = (P(None, ("stn", "sec"), None), P(), P(), P(), P(), P(), P(), P())
    out_specs = (P(("stn", "sec"), None, None, None), P(("stn", "sec"), None, None, None))
    return jax.shard_map(
        per_device, mesh=mesh, in_specs=in_specs, out_specs=out_specs, check_vma=False
    )
```

profile of v0, /device:TPU:1, one launch (start us, length us, event | category | flops | bytes accessed | tf_op | source)
XLA Modules:
  0.0 348.5 jit_solution(4968068274849040461)
XLA Ops:
  0.6 1.8 fusion.60
  2.5 14.5 %reshape.175 = bf16[2,4,139,4096]{3,2,1,0:T(8,128)(2,1)} reshape(bf16[2,4,569344]{2,1,0:T(4,128)(2,1)} %param.8) | data formatting | bytes 18219008 | tf_op jit(solution)/shard_map/reshape | solution.py:33
  17.0 52.5 %add_convert_fusion = bf16[2,4,128,4096]{3,2,1,0:T(8,128)(2,1)} fusion(bf16[2,4,139,4096]{3,2,1,0:T(8,128)(2,1)} %reshape.175, f32[4096]{0:T(1024)S(1)} %bitcast.81, f32[4096]{0:T(1024)S(1)} %bitcast.82, f32[4096]{0:T(1024)S(1)} %bitcast.72, f32[4096]{0:T(1024)S(1)} %bitcast.73, f32[4096]{0:T(1024)S(1)} %bitcast.74, f32[4096]{0:T(1024)S(1)} %bitcast.75, ...), kind=kLoop, calls=%fused_computation.3 | loop fusion | flops 150994944 | bytes 109248512 | tf_op jit(solution)/shard_map/convert_element_type | solution.py:39
  69.5 0.0 copy-start.4
  69.5 0.0 copy-start.5
  69.5 4.0 %fusion.57 = (bf16[1,4,128,4096]{3,2,1,0:T(8,128)(2,1)S(1)}, bf16[1,4,128,4096]{3,2,1,0:T(8,128)(2,1)S(1)}) fusion(bf16[2,4,128,4096]{3,2,1,0:T(8,128)(2,1)} %add_convert_fusion), kind=kLoop, calls=%fused_computation.88 | loop fusion | bytes 16777216 | tf_op jit(solution)/shard_map/slice | solution.py:49
  73.5 0.0 copy-done.4
  73.5 0.0 copy-done.5
  73.5 0.0 copy-start
  73.6 31.8 %fusion.11 = f32[512,512]{1,0:T(8,128)S(1)} fusion(bf16[512,4096]{1,0:T(8,128)(2,1)S(1)} %bitcast.67, s32[512]{0:T(512)S(1)} %pad_add_fusion), kind=kOutput, calls=%fused_computation.21 | convolution fusion | flops 2181038080 | bytes 5244928 | tf_op jit(solution)/shard_map/dot_general | solution.py:44
  105.4 0.0 copy-done
  105.4 32.4 %fusion.10 = f32[512,512]{1,0:T(8,128)} fusion(bf16[512,4096]{1,0:T(8,128)(2,1)S(1)} %bitcast.69, s32[512]{0:T(512)S(1)} %pad_add_fusion), kind=kOutput, calls=%fused_computation.20 | convolution fusion | flops 2181038080 | bytes 5244928 | tf_op jit(solution)/shard_map/dot_general | solution.py:44
  137.7 32.1 %fusion.17 = f32[512,512]{1,0:T(8,128)S(1)} fusion(f32[512,512]{1,0:T(8,128)S(1)} %fusion.11, bf16[512,4096]{1,0:T(8,128)(2,1)S(1)} %bitcast.70, s32[512]{0:T(512)S(1)} %pad_add_fusion), kind=kOutput, calls=%fused_computation.29 | convolution fusion | flops 2181300224 | bytes 6293504 | tf_op jit(solution)/shard_map/dot_general | solution.py:44
  169.8 0.4 concatenate.56
  170.2 0.0 copy-start.2
  170.2 0.0 copy-start.3
  170.2 34.4 %fusion.18 = f32[512,512]{1,0:T(8,128)S(1)} fusion(f32[512,512]{1,0:T(8,128)} %fusion.10, bf16[512,4096]{1,0:T(8,128)(2,1)} %bitcast.68, s32[512]{0:T(512)S(1)} %pad_add_fusion), kind=kOutput, calls=%fused_computation.30 | convolution fusion | flops 2181300224 | bytes 6293504 | tf_op jit(solution)/shard_map/dot_general | solution.py:44
  204.7 0.0 copy-start.1
  204.7 0.0 copy-start.6
  204.7 0.4 concatenate.57
  205.0 0.0 copy-done.2
  205.1 0.1 concatenate.59
  205.2 0.0 copy-done.3
  205.2 0.1 concatenate.60
  205.3 0.1 copy.37
  205.4 0.7 fusion.14
  206.1 41.5 %all_to_all.33 = bf16[2,64,4,1,1,4,256]{6,5,2,0,4,3,1:T(4,128)(2,1)S(1)} all-to-all(bf16[2,64,4,1,1,4,256]{6,5,2,0,4,3,1:T(4,128)(2,1)S(1)} %fusion.14), channel_id=1, replica_groups=mesh['stn'=64,'sec'=4] {'stn'}, dimensions={1} | all-to-all | bytes 2097152 | tf_op jit(solution)/shard_map/all_to_all | solution.py:87
  247.6 1.4 copy.38
  249.0 4.0 %all-to-all-start.1 = ((bf16[2,1,4,64,1,4,256]{6,5,3,0,4,1,2:T(4,128)(2,1)}), bf16[2,1,4,64,1,4,256]{6,5,3,0,4,1,2:T(4,128)(2,1)S(1)}, u32[]{:S(2)}, u32[]{:S(2)}) async-start(bf16[2,1,4,64,1,4,256]{6,5,3,0,4,1,2:T(4,128)(2,1)} %copy.38), calls=%async_computation.1 | async-start | bytes 2097152 | tf_op jit(solution)/shard_map/all_to_all | solution.py:86
  253.0 0.0 copy-done.1
  253.0 0.2 multiply_bitcast_fusion.1
  253.2 0.0 copy-done.6
  253.2 3.2 fusion
  256.4 3.2 fusion.1
  259.6 8.3 %all-to-all-done.1 = bf16[2,1,4,64,1,4,256]{6,5,3,0,4,1,2:T(4,128)(2,1)S(1)} async-done(((bf16[2,1,4,64,1,4,256]{6,5,3,0,4,1,2:T(4,128)(2,1)}), bf16[2,1,4,64,1,4,256]{6,5,3,0,4,1,2:T(4,128)(2,1)S(1)}, u32[]{:S(2)}, u32[]{:S(2)}) %all-to-all-start.1) | async-done | bytes 1048608 | tf_op jit(solution)/shard_map/all_to_all | solution.py:86
  267.9 0.4 fusion.58
  268.3 0.2 copy.40
  268.5 0.3 reshape.176
  268.7 0.2 convolution_bitcast_fusion
  268.9 0.2 convolution_bitcast_fusion.1
  269.1 0.2 copy.39
  269.3 0.1 squeeze.3
  269.4 0.1 fusion.59
  269.5 0.1 multiply_reduce_fusion
  269.6 0.7 fusion.15
  270.4 74.1 %psum.7 = f32[16]{0:T(128)S(1)} all-reduce(f32[16]{0:T(128)S(1)} %multiply_reduce_fusion), channel_id=1, replica_groups=mesh['stn'=64,'sec'=4] {'stn','sec'}, use_global_device_ids=true, to_apply=%region_1.2 | all-reduce | flops 16 | bytes 128 | tf_op jit(solution)/shard_map/psum | solution.py:102
  344.4 0.1 multiply_convert_fusion.12
  344.5 0.6 copy.43
  345.1 0.7 fusion.16
  345.9 2.4 pad_maximum_fusion
  (4 shorter events, 0.0 us)
Async XLA Ops:
  69.5 4.0 %copy-start.4 = (s32[256]{0:T(256)S(1)}, s32[256]{0:T(256)}, u32[]{:S(2)}) copy-start(s32[256]{0:T(256)} %param.11) | copy-start | bytes 3076
  69.5 4.0 %copy-start.5 = (s32[256]{0:T(256)S(1)}, s32[256]{0:T(256)}, u32[]{:S(2)}) copy-start(s32[256]{0:T(256)} %param.10) | copy-start | bytes 3076
  73.5 31.8 %copy-start = (bf16[1,4,128,4096]{3,2,1,0:T(8,128)(2,1)}, bf16[1,4,128,4096]{3,2,1,0:T(8,128)(2,1)S(1)}, u32[]{:S(2)}) copy-start(bf16[1,4,128,4096]{3,2,1,0:T(8,128)(2,1)S(1)} %get-tuple-element.12) | copy-start | bytes 12582916
  170.2 34.8 %copy-start.2 = (f32[256]{0:T(256)S(1)}, f32[256]{0:T(256)}, u32[]{:S(2)}) copy-start(f32[256]{0:T(256)} %param.12) | copy-start | bytes 3076
  170.2 35.0 %copy-start.3 = (f32[256]{0:T(256)S(1)}, f32[256]{0:T(256)}, u32[]{:S(2)}) copy-start(f32[256]{0:T(256)} %param.13) | copy-start | bytes 3076
  204.7 48.4 %copy-start.1 = (s32[16,512]{1,0:T(8,128)S(1)}, s32[16,512]{1,0:T(8,128)}, u32[]{:S(2)}) copy-start(s32[16,512]{1,0:T(8,128)} %param.15) | copy-start | bytes 98308
  204.7 48.5 %copy-start.6 = (s32[16,512]{1,0:T(8,128)S(1)}, s32[16,512]{1,0:T(8,128)}, u32[]{:S(2)}) copy-start(s32[16,512]{1,0:T(8,128)} %param.14) | copy-start | bytes 98308
  249.0 18.9 %all-to-all-start.1 = ((bf16[2,1,4,64,1,4,256]{6,5,3,0,4,1,2:T(4,128)(2,1)}), bf16[2,1,4,64,1,4,256]{6,5,3,0,4,1,2:T(4,128)(2,1)S(1)}, u32[]{:S(2)}, u32[]{:S(2)}) async-start(bf16[2,1,4,64,1,4,256]{6,5,3,0,4,1,2:T(4,128)(2,1)} %copy.38), calls=%async_computation.1 | async-start | bytes 2097152 | tf_op jit(solution)/shard_map/all_to_all | solution.py:86
where the time goes:
time: 352 us; the launch traced here: 348 us
  matrix products  139 us (39%)
  blocking collectives  116 us (33%)
  other arithmetic  56.1 us (16%)
  local copies, waits for them, and re-layouts  24.4 us (7%)
  waiting for transfers between devices  8.26 us (2%)
  starting transfers between devices  4.03 us (1%)
    dot_general x6, matrix products, contract(): lax.dot_general(left_rows, right_rows, contract_dims, preferred_element_t...  132 us
    psum x1, blocking collectives, per_device(): summed_power = lax.psum(local_power, ('stn', 'sec'))  74.1 us
    convert_element_type x1, other arithmetic, polyphase(): return summed.astype(jnp.bfloat16)  52.5 us
    all_to_all x1, blocking collectives, per_device(): lax.all_to_all(outgoing, 'stn', split_axis=1, concat_axis=3, tiled=True)  41.5 us
    reshape x1, local copies, waits for them, and re-layouts, polyphase(): framed = in_block.reshape(in_block.shape[0], in_block.shape[1], -1, points)  14.5 us
    all_to_all x1, waiting for transfers between devices, per_device(): lax.all_to_all(lax.all_to_all(outgoing, 'stn', split_axis=1, concat_axis=...  8.26 us
  transfers between devices with their start and end apart: 1, of which 1 were waited for; matrix products, arithmetic and copies ran while one was open for 2% of the time, Pallas kernels for 0%

commit v1 on v0

--- a/solution.py
+++ b/solution.py
@@ -99,7 +99,7 @@
     visibilities = jnp.stack([vis_re, vis_im])[None].astype(jnp.bfloat16)
     raw_beams = form_beams(beam_data, weight_re, weight_im)
     local_power = jnp.sum(raw_beams * raw_beams, axis=(0, 2, 3))
-    summed_power = lax.psum(local_power, ("stn", "sec"))
+    summed_power = jnp.sum(lax.all_gather(local_power, ("stn", "sec")), axis=0)
     beam_power = summed_power / (device_count * raw_beams.shape[2] * raw_beams.shape[3])
     beams = (raw_beams * lax.rsqrt(beam_power + epsilon)[None, :, None, None]).astype(jnp.bfloat16)
     return (visibilities, beams)

time: 352 us -> 356 us (1.011)
    unnamed x0 -> x1, blocking collectives: none -> 74.1 us
    psum x1 -> x0, blocking collectives: 74.1 us -> none  [per_device(): summed_power = lax.psum(local_power, ('stn', 'sec'))]
where the time goes in v1:
time: 356 us; the launch traced here: 353 us
  matrix products  140 us (39%)
  blocking collectives  116 us (33%)
  other arithmetic  56.8 us (16%)
  local copies, waits for them, and re-layouts  27.1 us (8%)
  waiting for transfers between devices  8.26 us (2%)
  starting transfers between devices  4.03 us (1%)
    dot_general x6, matrix products, contract(): lax.dot_general(left_rows, right_rows, contract_dims, preferred_element_t...  133 us
    unnamed x1, blocking collectives  74.1 us
    convert_element_type x1, other arithmetic, polyphase(): return summed.astype(jnp.bfloat16)  52.4 us
    all_to_all x1, blocking collectives, per_device(): lax.all_to_all(outgoing, 'stn', split_axis=1, concat_axis=3, tiled=True)  41.5 us
    reshape x1, local copies, waits for them, and re-layouts, polyphase(): framed = in_block.reshape(in_block.shape[0], in_block.shape[1], -1, points)  14.5 us
    all_to_all x1, waiting for transfers between devices, per_device(): lax.all_to_all(lax.all_to_all(outgoing, 'stn', split_axis=1, concat_axis=...  8.26 us
  transfers between devices with their start and end apart: 1, of which 1 were waited for; matrix products, arithmetic and copies ran while one was open for 2% of the time, Pallas kernels for 0%

profile of v1, /device:TPU:1, one launch (start us, length us, event | category | flops | bytes accessed | tf_op | source)
XLA Modules:
  0.0 352.8 jit_solution(5833188282569066548)
XLA Ops:
  0.6 1.8 fusion.60
  2.5 14.5 %reshape.179 = bf16[2,4,139,4096]{3,2,1,0:T(8,128)(2,1)} reshape(bf16[2,4,569344]{2,1,0:T(4,128)(2,1)} %param.8) | data formatting | bytes 18219008 | tf_op jit(solution)/shard_map/reshape | solution.py:33
  17.0 52.4 %add_convert_fusion = bf16[2,4,128,4096]{3,2,1,0:T(8,128)(2,1)} fusion(bf16[2,4,139,4096]{3,2,1,0:T(8,128)(2,1)} %reshape.179, f32[4096]{0:T(1024)S(1)} %bitcast.81, f32[4096]{0:T(1024)S(1)} %bitcast.82, f32[4096]{0:T(1024)S(1)} %bitcast.72, f32[4096]{0:T(1024)S(1)} %bitcast.73, f32[4096]{0:T(1024)S(1)} %bitcast.74, f32[4096]{0:T(1024)S(1)} %bitcast.75, ...), kind=kLoop, calls=%fused_computation.3 | loop fusion | flops 150994944 | bytes 109248512 | tf_op jit(solution)/shard_map/convert_element_type | solution.py:39
  69.4 0.0 copy-start.4
  69.4 0.0 copy-start.5
  69.4 4.0 %fusion.57 = (bf16[1,4,128,4096]{3,2,1,0:T(8,128)(2,1)S(1)}, bf16[1,4,128,4096]{3,2,1,0:T(8,128)(2,1)S(1)}) fusion(bf16[2,4,128,4096]{3,2,1,0:T(8,128)(2,1)} %add_convert_fusion), kind=kLoop, calls=%fused_computation.88 | loop fusion | bytes 16777216 | tf_op jit(solution)/shard_map/slice | solution.py:49
  73.4 0.0 copy-done.4
  73.4 0.0 copy-done.5
  73.4 0.0 copy-start
  73.4 31.8 %fusion.11 = f32[512,512]{1,0:T(8,128)S(1)} fusion(bf16[512,4096]{1,0:T(8,128)(2,1)S(1)} %bitcast.67, s32[512]{0:T(512)S(1)} %pad_add_fusion), kind=kOutput, calls=%fused_computation.21 | convolution fusion | flops 2181038080 | bytes 5244928 | tf_op jit(solution)/shard_map/dot_general | solution.py:44
  105.3 0.0 copy-done
  105.3 32.4 %fusion.10 = f32[512,512]{1,0:T(8,128)} fusion(bf16[512,4096]{1,0:T(8,128)(2,1)S(1)} %bitcast.69, s32[512]{0:T(512)S(1)} %pad_add_fusion), kind=kOutput, calls=%fused_computation.20 | convolution fusion | flops 2181038080 | bytes 5244928 | tf_op jit(solution)/shard_map/dot_general | solution.py:44
  137.6 32.1 %fusion.17 = f32[512,512]{1,0:T(8,128)S(1)} fusion(f32[512,512]{1,0:T(8,128)S(1)} %fusion.11, bf16[512,4096]{1,0:T(8,128)(2,1)S(1)} %bitcast.70, s32[512]{0:T(512)S(1)} %pad_add_fusion), kind=kOutput, calls=%fused_computation.29 | convolution fusion | flops 2181300224 | bytes 6293504 | tf_op jit(solution)/shard_map/dot_general | solution.py:44
  169.7 0.4 concatenate.56
  170.1 0.0 copy-start.2
  170.1 0.0 copy-start.3
  170.1 34.4 %fusion.18 = f32[512,512]{1,0:T(8,128)S(1)} fusion(f32[512,512]{1,0:T(8,128)} %fusion.10, bf16[512,4096]{1,0:T(8,128)(2,1)} %bitcast.68, s32[512]{0:T(512)S(1)} %pad_add_fusion), kind=kOutput, calls=%fused_computation.30 | convolution fusion | flops 2181300224 | bytes 6293504 | tf_op jit(solution)/shard_map/dot_general | solution.py:44
  204.5 0.0 copy-start.1
  204.6 0.0 copy-start.6
  204.6 0.4 concatenate.57
  204.9 0.0 copy-done.2
  205.0 0.1 concatenate.59
  205.1 0.0 copy-done.3
  205.1 0.1 concatenate.60
  205.2 0.1 copy.37
  205.3 0.7 fusion.14
  206.0 41.5 %all_to_all.33 = bf16[2,64,4,1,1,4,256]{6,5,2,0,4,3,1:T(4,128)(2,1)S(1)} all-to-all(bf16[2,64,4,1,1,4,256]{6,5,2,0,4,3,1:T(4,128)(2,1)S(1)} %fusion.14), channel_id=1, replica_groups=mesh['stn'=64,'sec'=4] {'stn'}, dimensions={1} | all-to-all | bytes 2097152 | tf_op jit(solution)/shard_map/all_to_all | solution.py:87
  247.5 1.4 copy.38
  248.9 4.0 %all-to-all-start.1 = ((bf16[2,1,4,64,1,4,256]{6,5,3,0,4,1,2:T(4,128)(2,1)}), bf16[2,1,4,64,1,4,256]{6,5,3,0,4,1,2:T(4,128)(2,1)S(1)}, u32[]{:S(2)}, u32[]{:S(2)}) async-start(bf16[2,1,4,64,1,4,256]{6,5,3,0,4,1,2:T(4,128)(2,1)} %copy.38), calls=%async_computation.1 | async-start | bytes 2097152 | tf_op jit(solution)/shard_map/all_to_all | solution.py:86
  252.9 0.0 copy-done.1
  252.9 0.2 multiply_bitcast_fusion.1
  253.1 0.0 copy-done.6
  253.1 3.2 fusion
  256.3 3.2 fusion.1
  259.5 8.3 %all-to-all-done.1 = bf16[2,1,4,64,1,4,256]{6,5,3,0,4,1,2:T(4,128)(2,1)S(1)} async-done(((bf16[2,1,4,64,1,4,256]{6,5,3,0,4,1,2:T(4,128)(2,1)}), bf16[2,1,4,64,1,4,256]{6,5,3,0,4,1,2:T(4,128)(2,1)S(1)}, u32[]{:S(2)}, u32[]{:S(2)}) %all-to-all-start.1) | async-done | bytes 1048608 | tf_op jit(solution)/shard_map/all_to_all | solution.py:86
  267.8 0.4 fusion.58
  268.2 0.2 copy.39
  268.4 0.1 squeeze.3
  268.5 0.8 fusion.59
  269.3 0.7 fusion.15
  270.0 1.0 copy.40
  271.0 1.8 reshape.180
  272.8 0.2 convolution_bitcast_fusion
  273.0 0.2 convolution_bitcast_fusion.1
  273.2 0.1 multiply_reduce_fusion
  273.3 0.3 dynamic-update-slice
  273.6 74.1 %all-reduce = f32[4096]{0:T(1024)S(1)} all-reduce(f32[4096]{0:T(1024)S(1)} %dynamic-update-slice), channel_id=2, replica_groups=mesh['stn'=64,'sec'=4] {'stn','sec'}, use_global_device_ids=true, to_apply=%add | all-reduce | flops 4096 | bytes 32768
  347.7 0.1 reshape.181
  347.8 0.1 reduce_sum.19
  347.8 0.1 multiply_convert_fusion.12
  347.9 0.6 copy.43
  348.5 1.7 fusion.16
  350.2 2.4 pad_maximum_fusion
  (5 shorter events, 0.0 us)
Async XLA Ops:
  69.4 4.0 %copy-start.4 = (s32[256]{0:T(256)S(1)}, s32[256]{0:T(256)}, u32[]{:S(2)}) copy-start(s32[256]{0:T(256)} %param.11) | copy-start | bytes 3076
  69.4 4.0 %copy-start.5 = (s32[256]{0:T(256)S(1)}, s32[256]{0:T(256)}, u32[]{:S(2)}) copy-start(s32[256]{0:T(256)} %param.10) | copy-start | bytes 3076
  73.4 31.8 %copy-start = (bf16[1,4,128,4096]{3,2,1,0:T(8,128)(2,1)}, bf16[1,4,128,4096]{3,2,1,0:T(8,128)(2,1)S(1)}, u32[]{:S(2)}) copy-start(bf16[1,4,128,4096]{3,2,1,0:T(8,128)(2,1)S(1)} %get-tuple-element.12) | copy-start | bytes 12582916
  170.1 34.8 %copy-start.2 = (f32[256]{0:T(256)S(1)}, f32[256]{0:T(256)}, u32[]{:S(2)}) copy-start(f32[256]{0:T(256)} %param.12) | copy-start | bytes 3076
  170.1 35.0 %copy-start.3 = (f32[256]{0:T(256)S(1)}, f32[256]{0:T(256)}, u32[]{:S(2)}) copy-start(f32[256]{0:T(256)} %param.13) | copy-start | bytes 3076
  204.5 48.4 %copy-start.1 = (s32[16,512]{1,0:T(8,128)S(1)}, s32[16,512]{1,0:T(8,128)}, u32[]{:S(2)}) copy-start(s32[16,512]{1,0:T(8,128)} %param.15) | copy-start | bytes 98308
  204.6 48.5 %copy-start.6 = (s32[16,512]{1,0:T(8,128)S(1)}, s32[16,512]{1,0:T(8,128)}, u32[]{:S(2)}) copy-start(s32[16,512]{1,0:T(8,128)} %param.14) | copy-start | bytes 98308
  248.9 18.9 %all-to-all-start.1 = ((bf16[2,1,4,64,1,4,256]{6,5,3,0,4,1,2:T(4,128)(2,1)}), bf16[2,1,4,64,1,4,256]{6,5,3,0,4,1,2:T(4,128)(2,1)S(1)}, u32[]{:S(2)}, u32[]{:S(2)}) async-start(bf16[2,1,4,64,1,4,256]{6,5,3,0,4,1,2:T(4,128)(2,1)} %copy.38), calls=%async_computation.1 | async-start | bytes 2097152 | tf_op jit(solution)/shard_map/all_to_all | solution.py:86
